TPU v7x, 32 devices: a whole 2x2x4 slice. The times are simulated.
32 devices in a mesh: img: 8 (over z, core), slab: 4 (over y, x).
Axes of the slice: x: 2, y: 2, z: 4, core: 2. Of those that a mesh axis runs over, the one named last changes fastest.
Arguments:
- image_masses: float32 [8, 3072, 3072], P('img', 'slab'), may hold values from 0.1 to 10
- dual_multipliers: float32 [8, 3072, 3072], P('img', 'slab'), may hold values from 0.1 to 10
- fraction_tops: int32 [8], P('img'), may hold values from 1 to 8
- banded_submatrices: bfloat16 [24, 3, 128, 128], replicated, as said below
- band_starts: int32 [24, 3], replicated, may hold values from -2 to 2, as said below
Outputs:
- barycenter: float32 [3072, 3072], P('slab')
- new_scalings: float32 [8, 3072, 3072], P('img', 'slab')
Inputs may be any that keep to these rules, and one draw needn't show every extreme that they name: `band_starts`: each row of offsets holds three consecutive numbers in increasing order; the first row is 0, 1, 2 and the last row is -2, -1, 0. `banded_submatrices`: all entries are positive.
All inputs are finite; a program needn't handle non-finite values.
Results may differ from a plain program's by a relative error of at most 0.0032.
Values may be sent and summed in bfloat16 or wider, within the bound.
No kernel may reach another device: no remote copies, remote signals or barrier semaphores. Data moves between devices by JAX's collectives and lax.ppermute only.
A program may use at most 192 MiB of HBM per device.

v0:
```python
import jax
import jax.numpy as jnp
from jax import lax
from jax.sharding import PartitionSpec as P

ITERS = 2


def offset_terms(banded_submatrices, band_starts):
    offsets = jnp.arange(-2, 3, dtype=jnp.int32)
    matches = band_starts[:, None, :] == offsets[None, :, None]
    picked = jnp.where(
        matches[:, :, :, None, None], banded_submatrices[:, None], jnp.zeros((), jnp.bfloat16)
    )
    return jnp.sum(picked, axis=2)


def column_sweep(field, terms):
    block_stack = terms.shape[0]
    width = terms.shape[2]
    count = field.shape[0]
    height = field.shape[1]
    leading = field.reshape((count * height, block_stack, width)).transpose(1, 0, 2)
    padded = jnp.pad(leading, ((2, 2), (0, 0), (0, 0)))
    total = jnp.zeros((block_stack, count * height, width), jnp.float32)
    for offset in range(5):
        total = total + lax.dot_general(
            padded[offset : offset + block_stack],
            terms[:, offset],
            (((2,), (2,)), ((0,), (0,))),
            preferred_element_type=jnp.float32,
        )
    return total.transpose(1, 0, 2).reshape((count, height, block_stack * width))


def rows_pass(padded, terms):
    block_stack = terms.shape[0]
    width = terms.shape[2]
    columns = padded.shape[2]
    split = padded[0].reshape((block_stack + 4, width, columns))
    total = jnp.zeros((block_stack, width, columns), jnp.float32)
    for offset in range(5):
        total = total + lax.dot_general(
            terms[:, offset],
            split[offset : offset + block_stack],
            (((2,), (1,)), ((0,), (0,))),
            preferred_element_type=jnp.float32,
        )
    outputs = [total.reshape((block_stack * width, columns))]
    return jnp.stack(outputs, axis=0)


def per_device(image_masses, dual_multipliers, fraction_tops, banded_submatrices, band_starts):
    width = banded_submatrices.shape[2]
    terms = offset_terms(banded_submatrices, band_starts)
    total_weight = lax.psum(jnp.sum(fraction_tops).astype(jnp.float32), "img")
    weights = fraction_tops.astype(jnp.float32)

    def apply_kernel(field):
        inner = column_sweep(field, terms).astype(jnp.bfloat16)
        columns = lax.all_to_all(inner, "slab", split_axis=2, concat_axis=1, tiled=True)
        padded = jnp.pad(columns, ((0, 0), (2 * width, 2 * width), (0, 0)))
        result = rows_pass(padded, terms).astype(jnp.bfloat16)
        return lax.all_to_all(result, "slab", split_axis=1, concat_axis=2, tiled=True)

    latest_multiplier = dual_multipliers
    barycenter = jnp.zeros(image_masses.shape[1:], jnp.float32)
    for iteration in range(ITERS):
        kernel_v = apply_kernel(latest_multiplier.astype(jnp.bfloat16))
        scaled_u = (image_masses / kernel_v.astype(jnp.float32)).astype(jnp.bfloat16)
        kernel_u = apply_kernel(scaled_u)
        value_portion = jnp.einsum("i,irc->rc", weights, jnp.log(kernel_u.astype(jnp.float32)))
        barycenter = jnp.exp(lax.psum(value_portion, "img") / total_weight)
        latest_multiplier = barycenter[None] / kernel_u.astype(jnp.float32)
    return (barycenter, latest_multiplier)


def solution(mesh):
    placed = (P("img", "slab", None), P("img", "slab", None), P("img"), P(), P())
    return jax.shard_map(
        per_device,
        mesh=mesh,
        in_specs=placed,
        out_specs=(P("slab", None), P("img", "slab", None)),
        check_vma=False,
    )
```

profile of v0, /device:TPU:0, one launch (start us, length us, event | category | flops | bytes accessed | tf_op | source)
XLA Modules:
  0.0 2068.6 jit_solution(6369687439953317268)
XLA Ops:
  77.7 49.0 %reduce.1 = bf16[3072,768]{1,0:T(8,128)(2,1)} reduce(bf16[3072,1,768]{2,1,0:T(2,128)(2,1)} %bitcast.287, bf16[]{:T(256)} %broadcast.49), dimensions={1}, to_apply=%bitcast.273.reduce_sub_computation | reduce | bytes 9437186
  132.1 61.0 %all_to_all.108 = bf16[4,2,294912]{2,1,0:T(2,128)(2,1)} all-to-all(bf16[4,2,294912]{2,1,0:T(2,128)(2,1)} %reshape.244), channel_id=1, replica_groups=mesh['img'=8,'slab'=4] {'slab'}, dimensions={0} | all-to-all | bytes 9437184 | tf_op jit(solution)/shard_map/all_to_all | solution.py:61
  269.0 49.2 %reduce.2 = bf16[3072,768]{1,0:T(8,128)(2,1)} reduce(bf16[3072,1,768]{2,1,0:T(2,128)(2,1)} %bitcast.290, bf16[]{:T(256)} %broadcast.49), dimensions={1}, to_apply=%bitcast.272.reduce_sub_computation | reduce | bytes 9437186
  338.2 42.8 %all-to-all-done.1 = bf16[4,2,294912]{2,1,0:T(2,128)(2,1)} async-done(((bf16[4,2,294912]{2,1,0:T(2,128)(2,1)}), bf16[4,2,294912]{2,1,0:T(2,128)(2,1)}, u32[]{:S(2)}, u32[]{:S(2)}) %all-to-all-start.1) | async-done | bytes 4718624 | tf_op jit(solution)/shard_map/all_to_all | solution.py:64
  389.0 23.5 %copy.138 = f32[1,4,768,768]{2,3,1,0:T(8,128)} copy(bf16[1,4,768,768]{3,0,2,1:T(2,128)(2,1)} %bitcast.291) | data formatting | bytes 14155776 | tf_op jit(solution)/shard_map/convert_element_type | solution.py:70
  478.4 49.4 %reduce.3 = bf16[3072,768]{1,0:T(8,128)(2,1)} reduce(bf16[3072,1,768]{2,1,0:T(2,128)(2,1)} %bitcast.292, bf16[]{:T(256)} %broadcast.49), dimensions={1}, to_apply=%bitcast.271.reduce_sub_computation | reduce | bytes 9437186
  533.1 58.9 %all_to_all.109 = bf16[4,2,294912]{2,1,0:T(2,128)(2,1)} all-to-all(bf16[4,2,294912]{2,1,0:T(2,128)(2,1)} %reshape.248), channel_id=1, replica_groups=mesh['img'=8,'slab'=4] {'slab'}, dimensions={0} | all-to-all | bytes 9437184 | tf_op jit(solution)/shard_map/all_to_all | solution.py:61
  667.7 49.1 %reduce.4 = bf16[3072,768]{1,0:T(8,128)(2,1)} reduce(bf16[3072,1,768]{2,1,0:T(2,128)(2,1)} %bitcast.294, bf16[]{:T(256)} %broadcast.49), dimensions={1}, to_apply=%bitcast.270.reduce_sub_computation | reduce | bytes 9437186
  727.9 50.3 %all-to-all-done.3 = bf16[4,2,294912]{2,1,0:T(2,128)(2,1)} async-done(((bf16[4,2,294912]{2,1,0:T(2,128)(2,1)}), bf16[4,2,294912]{2,1,0:T(2,128)(2,1)}, u32[]{:S(2)}, u32[]{:S(2)}) %all-to-all-start.3) | async-done | bytes 4718624 | tf_op jit(solution)/shard_map/all_to_all | solution.py:64
  801.7 23.3 %copy.145 = f32[1,4,768,768]{2,3,1,0:T(8,128)} copy(f32[1,4,768,768]{3,0,2,1:T(1,128)} %bitcast.302) | data formatting | bytes 18874368 | tf_op jit(solution)/shard_map/i,irc->rc/dot_general | solution.py:72
  841.9 23.6 %copy.146 = f32[1,4,768,768]{2,3,1,0:T(8,128)} copy(bf16[1,4,768,768]{3,0,2,1:T(2,128)(2,1)} %bitcast.274) | data formatting | bytes 14155776 | tf_op jit(solution)/shard_map/convert_element_type | solution.py:72
  865.5 155.0 %all-reduce.11.cloned.1.call-done = f32[768,3072]{0,1:T(8,128)} async-done(((f32[768,3072]{0,1:T(8,128)}), f32[768,3072]{0,1:T(8,128)}) %all-reduce.11.cloned.1.call-update) | async-done | bytes 9437200 | tf_op jit(solution)/shard_map/psum | solution.py:73
  1086.8 49.4 %reduce.5 = bf16[3072,768]{1,0:T(8,128)(2,1)} reduce(bf16[3072,1,768]{2,1,0:T(2,128)(2,1)} %bitcast.295, bf16[]{:T(256)} %broadcast.49), dimensions={1}, to_apply=%bitcast.269.reduce_sub_computation | reduce | bytes 9437186
  1141.6 59.5 %all_to_all.110 = bf16[4,2,294912]{2,1,0:T(2,128)(2,1)} all-to-all(bf16[4,2,294912]{2,1,0:T(2,128)(2,1)} %reshape.252), channel_id=1, replica_groups=mesh['img'=8,'slab'=4] {'slab'}, dimensions={0} | all-to-all | bytes 9437184 | tf_op jit(solution)/shard_map/all_to_all | solution.py:61
  1276.9 49.1 %reduce.6 = bf16[3072,768]{1,0:T(8,128)(2,1)} reduce(bf16[3072,1,768]{2,1,0:T(2,128)(2,1)} %bitcast.297, bf16[]{:T(256)} %broadcast.49), dimensions={1}, to_apply=%bitcast.268.reduce_sub_computation | reduce | bytes 9437186
  1331.4 58.2 %all_to_all.111 = bf16[4,2,294912]{2,1,0:T(2,128)(2,1)} all-to-all(bf16[4,2,294912]{2,1,0:T(2,128)(2,1)} %reshape.254), channel_id=1, replica_groups=mesh['img'=8,'slab'=4] {'slab'}, dimensions={0} | all-to-all | bytes 9437184 | tf_op jit(solution)/shard_map/all_to_all | solution.py:64
  1397.6 23.5 %copy.152 = f32[1,4,768,768]{2,3,1,0:T(8,128)} copy(bf16[1,4,768,768]{3,0,2,1:T(2,128)(2,1)} %bitcast.298) | data formatting | bytes 14155776 | tf_op jit(solution)/shard_map/convert_element_type | solution.py:70
  1486.9 49.4 %reduce.7 = bf16[3072,768]{1,0:T(8,128)(2,1)} reduce(bf16[3072,1,768]{2,1,0:T(2,128)(2,1)} %bitcast.299, bf16[]{:T(256)} %broadcast.49), dimensions={1}, to_apply=%bitcast.267.reduce_sub_computation | reduce | bytes 9437186
  1541.8 56.8 %all_to_all.112 = bf16[4,2,294912]{2,1,0:T(2,128)(2,1)} all-to-all(bf16[4,2,294912]{2,1,0:T(2,128)(2,1)} %reshape.256), channel_id=1, replica_groups=mesh['img'=8,'slab'=4] {'slab'}, dimensions={0} | all-to-all | bytes 9437184 | tf_op jit(solution)/shard_map/all_to_all | solution.py:61
  1674.4 49.2 %reduce.8 = bf16[3072,768]{1,0:T(8,128)(2,1)} reduce(bf16[3072,1,768]{2,1,0:T(2,128)(2,1)} %bitcast.288, bf16[]{:T(256)} %broadcast.49), dimensions={1}, to_apply=%bitcast.266.reduce_sub_computation | reduce | bytes 9437186
  1729.0 55.4 %all_to_all.113 = bf16[4,2,294912]{2,1,0:T(2,128)(2,1)} all-to-all(bf16[4,2,294912]{2,1,0:T(2,128)(2,1)} %reshape.258), channel_id=1, replica_groups=mesh['img'=8,'slab'=4] {'slab'}, dimensions={0} | all-to-all | bytes 9437184 | tf_op jit(solution)/shard_map/all_to_all | solution.py:64
  1807.7 23.3 %copy.159 = f32[1,4,768,768]{2,3,1,0:T(8,128)} copy(f32[1,4,768,768]{3,0,2,1:T(1,128)} %bitcast.301) | data formatting | bytes 18874368 | tf_op jit(solution)/shard_map/i,irc->rc/dot_general | solution.py:72
  1831.0 23.5 %copy.160 = f32[1,4,768,768]{2,3,1,0:T(8,128)} copy(bf16[1,4,768,768]{3,0,2,1:T(2,128)(2,1)} %bitcast.275) | data formatting | bytes 14155776 | tf_op jit(solution)/shard_map/convert_element_type | solution.py:72
  1854.5 172.9 %all-reduce.13.cloned.1.call-done = f32[768,3072]{0,1:T(8,128)} async-done(((f32[768,3072]{0,1:T(8,128)}), f32[768,3072]{0,1:T(8,128)}) %all-reduce.13.cloned.1.call-update) | async-done | bytes 9437200 | tf_op jit(solution)/shard_map/psum | solution.py:73
  (136 shorter events, 748.3 us)
Async XLA Ops:
  15.6 6.9 copy-start.16
  26.3 18.9 copy-start
  26.3 8.9 copy-start.12
  214.4 7.8 copy-start.8
  222.3 3.8 copy-start.1
  323.6 57.3 %all-to-all-start.1 = ((bf16[4,2,294912]{2,1,0:T(2,128)(2,1)}), bf16[4,2,294912]{2,1,0:T(2,128)(2,1)}, u32[]{:S(2)}, u32[]{:S(2)}) async-start(bf16[4,2,294912]{2,1,0:T(2,128)(2,1)} %reshape.246), calls=%async_computation.1 | async-start | bytes 9437184 | tf_op jit(solution)/shard_map/all_to_all | solution.py:64
  429.2 7.7 copy-start.2
  429.2 7.7 copy-start.13
  613.3 7.7 copy-start.9
  621.0 3.8 copy-start.3
  722.3 56.0 %all-to-all-start.3 = ((bf16[4,2,294912]{2,1,0:T(2,128)(2,1)}), bf16[4,2,294912]{2,1,0:T(2,128)(2,1)}, u32[]{:S(2)}, u32[]{:S(2)}) async-start(bf16[4,2,294912]{2,1,0:T(2,128)(2,1)} %reshape.250), calls=%async_computation.3 | async-start | bytes 9437184 | tf_op jit(solution)/shard_map/all_to_all | solution.py:64
  727.2 293.3 %all-reduce.11.cloned.1.call-start = ((), (), s32[]{:S(2)}) async-start(), calls=%async_computation.8 | async-start | bytes 18874368 | tf_op jit(solution)/shard_map/psum | solution.py:73
  824.9 1202.4 %all-reduce.13.cloned.1.call-start = ((), (), s32[]{:S(2)}) async-start(), calls=%async_computation.9 | async-start | bytes 18874368 | tf_op jit(solution)/shard_map/psum | solution.py:73
  1037.6 7.7 copy-start.4
  1037.6 7.7 copy-start.14
  1222.4 7.7 copy-start.10
  1230.1 3.8 copy-start.5
  1437.7 7.8 copy-start.6
  1437.7 7.8 copy-start.15
  1619.9 7.8 copy-start.11
  1627.7 3.8 copy-start.7
Sparse Core Ops, SparseCore 0:
  825.1 195.3 all-reduce.10
  1831.1 196.2 all-reduce.12
where the time goes:
time: 2080 us; the launch traced here: 2070 us
  other arithmetic  474 us (23%)
  local copies, waits for them, and re-layouts  458 us (22%)
  waiting for transfers between devices  421 us (20%)
  blocking collectives  367 us (18%)
  matrix products  324 us (16%)
    unnamed x8, other arithmetic  394 us
    psum x2, waiting for transfers between devices, per_device(): barycenter = jnp.exp(lax.psum(value_portion, 'img') / total_weight)  328 us
    all_to_all x4, blocking collectives, apply_kernel(): lax.all_to_all(inner, 'slab', split_axis=2, concat_axis=1, tiled=True)  236 us
    unnamed x60, local copies, waits for them, and re-layouts  174 us
    dot_general x20, matrix products, rows_pass(): lax.dot_general(terms[:, offset], split[offset:offset + block_stack], (((...  165 us
    dot_general x20, matrix products, column_sweep(): lax.dot_general(padded[offset:offset + block_stack], terms[:, offset], ((...  160 us
    all_to_all x2, blocking collectives, apply_kernel(): lax.all_to_all(result, 'slab', split_axis=1, concat_axis=2, tiled=True)  114 us
    all_to_all x2, waiting for transfers between devices, apply_kernel(): lax.all_to_all(result, 'slab', split_axis=1, concat_axis=2, tiled=True)  93.1 us
  transfers between devices with their start and end apart: 4, of which 4 were waited for; matrix products, arithmetic and copies ran while one was open for 3% of the time, Pallas kernels for 0%

commit v1 on v0

--- a/solution.py
+++ b/solution.py
@@ -4,6 +4,18 @@
 from jax.sharding import PartitionSpec as P
 
 ITERS = 2
+
+
+def in_blocks(x, dim, size):
+    shape = x.shape
+    blocks = x.reshape(*shape[:dim], size, shape[dim] // size, *shape[dim + 1 :])
+    return jnp.moveaxis(blocks, dim, 0)
+
+
+def laid_out(blocks, dim):
+    lengths = list(blocks.shape[1:])
+    lengths[dim] *= blocks.shape[0]
+    return jnp.moveaxis(blocks, 0, dim).reshape(lengths)
 
 
 def offset_terms(banded_submatrices, band_starts):
@@ -58,7 +70,14 @@
 
     def apply_kernel(field):
         inner = column_sweep(field, terms).astype(jnp.bfloat16)
-        columns = lax.all_to_all(inner, "slab", split_axis=2, concat_axis=1, tiled=True)
+        peers, index = (lax.axis_size("slab"), lax.axis_index("slab"))
+        blocks = in_blocks(inner, 2, peers)
+        outs = [blocks[index]]
+        for step in range(1, peers):
+            sent = blocks[index ^ step]
+            outs.append(lax.ppermute(sent, "slab", [(i, i ^ step) for i in range(peers)]))
+        blocks = jnp.stack(outs)[index ^ jnp.arange(peers)]
+        columns = laid_out(blocks, 1)
         padded = jnp.pad(columns, ((0, 0), (2 * width, 2 * width), (0, 0)))
         result = rows_pass(padded, terms).astype(jnp.bfloat16)
         return lax.all_to_all(result, "slab", split_axis=1, concat_axis=2, tiled=True)

time: 2080 us -> 1800 us (0.87)
  blocking collectives: 367 us -> 134 us
  waiting for transfers between devices: 421 us -> 614 us
  other arithmetic: 474 us -> 291 us
  local copies, waits for them, and re-layouts: 458 us -> 389 us
    all_to_all x4 -> x0, blocking collectives: 236 us -> none  [apply_kernel(): lax.all_to_all(inner, 'slab', split_axis=2, concat_axis=1, tiled=True)]
    unnamed x8 -> x4, other arithmetic: 394 us -> 196 us
    ppermute x0 -> x12, waiting for transfers between devices: none -> 195 us  [apply_kernel(): lax.ppermute(sent, 'slab', [(i, i ^ step) for i in range(peers)])]
    unnamed x60 -> x42, local copies, waits for them, and re-layouts: 174 us -> 91.9 us
    convert_element_type x4 -> x0, local copies, waits for them, and re-layouts: 38.6 us -> none  [apply_kernel(): inner = column_sweep(field, terms).astype(jnp.bfloat16)]
    another operation x0 -> x20, local copies, waits for them, and re-layouts: none -> 38.4 us
    all_to_all x4 -> x0, local copies, waits for them, and re-layouts: 26.4 us -> none  [apply_kernel(): lax.all_to_all(inner, 'slab', split_axis=2, concat_axis=1, tiled=True)]
    gather x0 -> x4, local copies, waits for them, and re-layouts: none -> 21.8 us  [apply_kernel(): blocks = jnp.stack(outs)[index ^ jnp.arange(peers)]]
  transfers between devices with their start and end apart: 4 -> 16, of which waited for: 4 -> 13; matrix products, arithmetic and copies ran while one was open for 3% -> 3% of each run, Pallas kernels for 0% -> 0%
where the time goes in v1:
time: 1800 us; the launch traced here: 1780 us
  waiting for transfers between devices  614 us (34%)
  local copies, waits for them, and re-layouts  389 us (22%)
  matrix products  314 us (17%)
  other arithmetic  291 us (16%)
  blocking collectives  134 us (7%)
  starting transfers between devices  25.3 us (1%)
    psum x2, waiting for transfers between devices, per_device(): barycenter = jnp.exp(lax.psum(value_portion, 'img') / total_weight)  326 us
    unnamed x4, other arithmetic  196 us
    ppermute x12, waiting for transfers between devices, apply_kernel(): lax.ppermute(sent, 'slab', [(i, i ^ step) for i in range(peers)])  195 us
    dot_general x20, matrix products, column_sweep(): lax.dot_general(padded[offset:offset + block_stack], terms[:, offset], ((...  160 us
    dot_general x20, matrix products, rows_pass(): lax.dot_general(terms[:, offset], split[offset:offset + block_stack], (((...  154 us
    all_to_all x2, blocking collectives, apply_kernel(): lax.all_to_all(result, 'slab', split_axis=1, concat_axis=2, tiled=True)  115 us
    all_to_all x2, waiting for transfers between devices, apply_kernel(): lax.all_to_all(result, 'slab', split_axis=1, concat_axis=2, tiled=True)  92.6 us
    unnamed x42, local copies, waits for them, and re-layouts  91.9 us
  transfers between devices with their start and end apart: 16, of which 13 were waited for; matrix products, arithmetic and copies ran while one was open for 3% of the time, Pallas kernels for 0%

profile of v1, /device:TPU:0, one launch (start us, length us, event | category | flops | bytes accessed | tf_op | source)
XLA Modules:
  0.0 1782.8 jit_solution(8484849492822830462)
XLA Ops:
  81.4 21.9 %collective-permute-done = bf16[1,768,768]{2,1,0:T(8,128)(2,1)} collective-permute-done((bf16[1,768,768]{2,1,0:T(8,128)(2,1)}, bf16[1,768,768]{2,1,0:T(8,128)(2,1)}, u32[]{:S(2)}, u32[]{:S(2)}) %collective-permute-start) | collective-permute-done | bytes 1179680 | tf_op jit(solution)/shard_map/ppermute | solution.py:78
  103.2 27.4 %collective-permute-done.1 = bf16[1,768,768]{2,1,0:T(8,128)(2,1)S(1)} collective-permute-done((bf16[1,768,768]{2,1,0:T(8,128)(2,1)}, bf16[1,768,768]{2,1,0:T(8,128)(2,1)S(1)}, u32[]{:S(2)}, u32[]{:S(2)}) %collective-permute-start.1) | collective-permute-done | bytes 1179680 | tf_op jit(solution)/shard_map/ppermute | solution.py:78
  196.2 49.0 %reduce.1 = bf16[3072,768]{1,0:T(8,128)(2,1)} reduce(bf16[3072,1,768]{2,1,0:T(2,128)(2,1)} %bitcast.297, bf16[]{:T(256)} %broadcast.90), dimensions={1}, to_apply=%bitcast.283.reduce_sub_computation | reduce | bytes 9437186
  265.6 42.5 %all-to-all-done = bf16[4,2,294912]{2,1,0:T(2,128)(2,1)} async-done(((bf16[4,2,294912]{2,1,0:T(2,128)(2,1)}), bf16[4,2,294912]{2,1,0:T(2,128)(2,1)}, u32[]{:S(2)}, u32[]{:S(2)}) %all-to-all-start) | async-done | bytes 4718624 | tf_op jit(solution)/shard_map/all_to_all | solution.py:83
  316.2 23.6 %copy.95 = f32[1,4,768,768]{2,3,1,0:T(8,128)} copy(bf16[1,4,768,768]{3,0,2,1:T(2,128)(2,1)} %bitcast.299) | data formatting | bytes 14155776 | tf_op jit(solution)/shard_map/convert_element_type | solution.py:89
  409.2 25.0 %collective-permute-done.3 = bf16[1,768,768]{2,1,0:T(8,128)(2,1)S(1)} collective-permute-done((bf16[1,768,768]{2,1,0:T(8,128)(2,1)}, bf16[1,768,768]{2,1,0:T(8,128)(2,1)S(1)}, u32[]{:S(2)}, u32[]{:S(2)}) %collective-permute-start.3) | collective-permute-done | bytes 1179680 | tf_op jit(solution)/shard_map/ppermute | solution.py:78
  434.2 23.4 %collective-permute-done.4 = bf16[1,768,768]{2,1,0:T(8,128)(2,1)} collective-permute-done((bf16[1,768,768]{2,1,0:T(8,128)(2,1)}, bf16[1,768,768]{2,1,0:T(8,128)(2,1)}, u32[]{:S(2)}, u32[]{:S(2)}) %collective-permute-start.4) | collective-permute-done | bytes 1179680 | tf_op jit(solution)/shard_map/ppermute | solution.py:78
  522.8 49.0 %reduce.2 = bf16[3072,768]{1,0:T(8,128)(2,1)} reduce(bf16[3072,1,768]{2,1,0:T(2,128)(2,1)} %bitcast.300, bf16[]{:T(256)} %broadcast.90), dimensions={1}, to_apply=%bitcast.282.reduce_sub_computation | reduce | bytes 9437186
  582.9 50.1 %all-to-all-done.1 = bf16[4,2,294912]{2,1,0:T(2,128)(2,1)} async-done(((bf16[4,2,294912]{2,1,0:T(2,128)(2,1)}), bf16[4,2,294912]{2,1,0:T(2,128)(2,1)}, u32[]{:S(2)}, u32[]{:S(2)}) %all-to-all-start.1) | async-done | bytes 4718624 | tf_op jit(solution)/shard_map/all_to_all | solution.py:83
  656.4 23.3 %copy.103 = f32[1,4,768,768]{2,3,1,0:T(8,128)} copy(f32[1,4,768,768]{3,0,2,1:T(1,128)} %bitcast.304) | data formatting | bytes 18874368 | tf_op jit(solution)/shard_map/i,irc->rc/dot_general | solution.py:91
  698.5 23.6 %copy.104 = f32[1,4,768,768]{2,3,1,0:T(8,128)} copy(bf16[1,4,768,768]{3,0,2,1:T(2,128)(2,1)} %bitcast.284) | data formatting | bytes 14155776 | tf_op jit(solution)/shard_map/convert_element_type | solution.py:91
  722.2 153.9 %all-reduce.11.cloned.1.call-done = f32[768,3072]{0,1:T(8,128)} async-done(((f32[768,3072]{0,1:T(8,128)}), f32[768,3072]{0,1:T(8,128)}) %all-reduce.11.cloned.1.call-update) | async-done | bytes 9437200 | tf_op jit(solution)/shard_map/psum | solution.py:92
  945.9 25.0 %collective-permute-done.6 = bf16[1,768,768]{2,1,0:T(8,128)(2,1)S(1)} collective-permute-done((bf16[1,768,768]{2,1,0:T(8,128)(2,1)}, bf16[1,768,768]{2,1,0:T(8,128)(2,1)S(1)}, u32[]{:S(2)}, u32[]{:S(2)}) %collective-permute-start.6) | collective-permute-done | bytes 1179680 | tf_op jit(solution)/shard_map/ppermute | solution.py:78
  970.8 25.2 %collective-permute-done.7 = bf16[1,768,768]{2,1,0:T(8,128)(2,1)} collective-permute-done((bf16[1,768,768]{2,1,0:T(8,128)(2,1)}, bf16[1,768,768]{2,1,0:T(8,128)(2,1)}, u32[]{:S(2)}, u32[]{:S(2)}) %collective-permute-start.7) | collective-permute-done | bytes 1179680 | tf_op jit(solution)/shard_map/ppermute | solution.py:78
  1061.3 49.0 %reduce.3 = bf16[3072,768]{1,0:T(8,128)(2,1)} reduce(bf16[3072,1,768]{2,1,0:T(2,128)(2,1)} %bitcast.301, bf16[]{:T(256)} %broadcast.90), dimensions={1}, to_apply=%bitcast.281.reduce_sub_computation | reduce | bytes 9437186
  1115.9 58.4 %all_to_all.16 = bf16[4,2,294912]{2,1,0:T(2,128)(2,1)} all-to-all(bf16[4,2,294912]{2,1,0:T(2,128)(2,1)} %reshape.348), channel_id=1, replica_groups=mesh['img'=8,'slab'=4] {'slab'}, dimensions={0} | all-to-all | bytes 9437184 | tf_op jit(solution)/shard_map/all_to_all | solution.py:83
  1182.4 23.6 %copy.111 = f32[1,4,768,768]{2,3,1,0:T(8,128)} copy(bf16[1,4,768,768]{3,0,2,1:T(2,128)(2,1)} %bitcast.302) | data formatting | bytes 14155776 | tf_op jit(solution)/shard_map/convert_element_type | solution.py:89
  1275.3 25.0 %collective-permute-done.9 = bf16[1,768,768]{2,1,0:T(8,128)(2,1)S(1)} collective-permute-done((bf16[1,768,768]{2,1,0:T(8,128)(2,1)}, bf16[1,768,768]{2,1,0:T(8,128)(2,1)S(1)}, u32[]{:S(2)}, u32[]{:S(2)}) %collective-permute-start.9) | collective-permute-done | bytes 1179680 | tf_op jit(solution)/shard_map/ppermute | solution.py:78
  1300.3 20.7 %collective-permute-done.10 = bf16[1,768,768]{2,1,0:T(8,128)(2,1)} collective-permute-done((bf16[1,768,768]{2,1,0:T(8,128)(2,1)}, bf16[1,768,768]{2,1,0:T(8,128)(2,1)}, u32[]{:S(2)}, u32[]{:S(2)}) %collective-permute-start.10) | collective-permute-done | bytes 1179680 | tf_op jit(solution)/shard_map/ppermute | solution.py:78
  1388.1 49.2 %reduce.4 = bf16[3072,768]{1,0:T(8,128)(2,1)} reduce(bf16[3072,1,768]{2,1,0:T(2,128)(2,1)} %bitcast.298, bf16[]{:T(256)} %broadcast.90), dimensions={1}, to_apply=%bitcast.280.reduce_sub_computation | reduce | bytes 9437186
  1442.7 56.6 %all_to_all.17 = bf16[4,2,294912]{2,1,0:T(2,128)(2,1)} all-to-all(bf16[4,2,294912]{2,1,0:T(2,128)(2,1)} %reshape.350), channel_id=1, replica_groups=mesh['img'=8,'slab'=4] {'slab'}, dimensions={0} | all-to-all | bytes 9437184 | tf_op jit(solution)/shard_map/all_to_all | solution.py:83
  1522.6 23.3 %copy.119 = f32[1,4,768,768]{2,3,1,0:T(8,128)} copy(f32[1,4,768,768]{3,0,2,1:T(1,128)} %bitcast.303) | data formatting | bytes 18874368 | tf_op jit(solution)/shard_map/i,irc->rc/dot_general | solution.py:91
  1545.9 23.5 %copy.120 = f32[1,4,768,768]{2,3,1,0:T(8,128)} copy(bf16[1,4,768,768]{3,0,2,1:T(2,128)(2,1)} %bitcast.285) | data formatting | bytes 14155776 | tf_op jit(solution)/shard_map/convert_element_type | solution.py:91
  1569.4 172.2 %all-reduce.13.cloned.1.call-done = f32[768,3072]{0,1:T(8,128)} async-done(((f32[768,3072]{0,1:T(8,128)}), f32[768,3072]{0,1:T(8,128)}) %all-reduce.13.cloned.1.call-update) | async-done | bytes 9437200 | tf_op jit(solution)/shard_map/psum | solution.py:92
  (156 shorter events, 703.3 us)
Async XLA Ops:
  26.3 19.0 %copy-start = (bf16[24,5,128,128]{3,2,1,0:T(8,128)(2,1)}, bf16[24,5,128,128]{3,2,1,0:T(8,128)(2,1)S(1)}, u32[]{:S(2)}) copy-start(bf16[24,5,128,128]{3,2,1,0:T(8,128)(2,1)S(1)} %select_reduce_fusion) | copy-start | bytes 11796484
  26.3 8.9 copy-start.8
  73.2 30.1 %collective-permute-start = (bf16[1,768,768]{2,1,0:T(8,128)(2,1)}, bf16[1,768,768]{2,1,0:T(8,128)(2,1)}, u32[]{:S(2)}, u32[]{:S(2)}) collective-permute-start(bf16[1,768,768]{2,1,0:T(8,128)(2,1)} %bitcast.344), channel_id=1, source_target_pairs={{0,1},{1,0},{2,3},{3,2},{4,5},{5,4},{6,7},{7,6},{8,9},{9,8},{10,11... | collective-permute-start | bytes 3538952 | tf_op jit(solution)/shard_map/ppermute | solution.py:78
  77.7 52.9 %collective-permute-start.1 = (bf16[1,768,768]{2,1,0:T(8,128)(2,1)}, bf16[1,768,768]{2,1,0:T(8,128)(2,1)S(1)}, u32[]{:S(2)}, u32[]{:S(2)}) collective-permute-start(bf16[1,768,768]{2,1,0:T(8,128)(2,1)} %bitcast.345), channel_id=1, source_target_pairs={{0,2},{1,3},{2,0},{3,1},{4,6},{5,7},{6,4},{7,5},{8,10},{9,11},{10,... | collective-permute-start | bytes 3538952 | tf_op jit(solution)/shard_map/ppermute | solution.py:78
  80.7 50.0 %collective-permute-start.2 = (bf16[1,768,768]{2,1,0:T(8,128)(2,1)}, bf16[1,768,768]{2,1,0:T(8,128)(2,1)}, u32[]{:S(2)}, u32[]{:S(2)}) collective-permute-start(bf16[1,768,768]{2,1,0:T(8,128)(2,1)} %bitcast.349), channel_id=1, source_target_pairs={{0,3},{1,2},{2,1},{3,0},{4,7},{5,6},{6,5},{7,4},{8,11},{9,10},{10,... | collective-permute-start | bytes 3538952 | tf_op jit(solution)/shard_map/ppermute | solution.py:78
  81.4 53.0 %copy-start.13 = (s32[1024]{0:T(1024)}, s32[1024]{0:T(1024)S(1)}, u32[]{:S(2)}) copy-start(s32[1024]{0:T(1024)S(1)} %pad_clamp_fusion) | copy-start | bytes 12292
  139.8 7.8 copy-start.1
  250.7 57.5 %all-to-all-start = ((bf16[4,2,294912]{2,1,0:T(2,128)(2,1)}), bf16[4,2,294912]{2,1,0:T(2,128)(2,1)}, u32[]{:S(2)}, u32[]{:S(2)}) async-start(bf16[4,2,294912]{2,1,0:T(2,128)(2,1)} %reshape.344), calls=%async_computation | async-start | bytes 9437184 | tf_op jit(solution)/shard_map/all_to_all | solution.py:83
  405.1 29.1 %collective-permute-start.3 = (bf16[1,768,768]{2,1,0:T(8,128)(2,1)}, bf16[1,768,768]{2,1,0:T(8,128)(2,1)S(1)}, u32[]{:S(2)}, u32[]{:S(2)}) collective-permute-start(bf16[1,768,768]{2,1,0:T(8,128)(2,1)} %bitcast.350), channel_id=1, source_target_pairs={{0,1},{1,0},{2,3},{3,2},{4,5},{5,4},{6,7},{7,6},{8,9},{9,8},{10,11... | collective-permute-start | bytes 3538952 | tf_op jit(solution)/shard_map/ppermute | solution.py:78
  406.5 51.1 %collective-permute-start.4 = (bf16[1,768,768]{2,1,0:T(8,128)(2,1)}, bf16[1,768,768]{2,1,0:T(8,128)(2,1)}, u32[]{:S(2)}, u32[]{:S(2)}) collective-permute-start(bf16[1,768,768]{2,1,0:T(8,128)(2,1)} %bitcast.346), channel_id=1, source_target_pairs={{0,2},{1,3},{2,0},{3,1},{4,6},{5,7},{6,4},{7,5},{8,10},{9,11},{10,... | collective-permute-start | bytes 3538952 | tf_op jit(solution)/shard_map/ppermute | solution.py:78
  407.1 50.5 %collective-permute-start.5 = (bf16[1,768,768]{2,1,0:T(8,128)(2,1)}, bf16[1,768,768]{2,1,0:T(8,128)(2,1)}, u32[]{:S(2)}, u32[]{:S(2)}) collective-permute-start(bf16[1,768,768]{2,1,0:T(8,128)(2,1)} %bitcast.341), channel_id=1, source_target_pairs={{0,3},{1,2},{2,1},{3,0},{4,7},{5,6},{6,5},{7,4},{8,11},{9,10},{10,... | collective-permute-start | bytes 3538952 | tf_op jit(solution)/shard_map/ppermute | solution.py:78
  466.9 7.9 copy-start.3
  577.2 55.8 %all-to-all-start.1 = ((bf16[4,2,294912]{2,1,0:T(2,128)(2,1)}), bf16[4,2,294912]{2,1,0:T(2,128)(2,1)}, u32[]{:S(2)}, u32[]{:S(2)}) async-start(bf16[4,2,294912]{2,1,0:T(2,128)(2,1)} %reshape.346), calls=%async_computation.1 | async-start | bytes 9437184 | tf_op jit(solution)/shard_map/all_to_all | solution.py:83
  582.2 293.9 %all-reduce.11.cloned.1.call-start = ((), (), s32[]{:S(2)}) async-start(), calls=%async_computation.4 | async-start | bytes 18874368 | tf_op jit(solution)/shard_map/psum | solution.py:92
  679.7 1061.8 %all-reduce.13.cloned.1.call-start = ((), (), s32[]{:S(2)}) async-start(), calls=%async_computation.5 | async-start | bytes 18874368 | tf_op jit(solution)/shard_map/psum | solution.py:92
  941.7 29.1 %collective-permute-start.6 = (bf16[1,768,768]{2,1,0:T(8,128)(2,1)}, bf16[1,768,768]{2,1,0:T(8,128)(2,1)S(1)}, u32[]{:S(2)}, u32[]{:S(2)}) collective-permute-start(bf16[1,768,768]{2,1,0:T(8,128)(2,1)} %bitcast.351), channel_id=1, source_target_pairs={{0,1},{1,0},{2,3},{3,2},{4,5},{5,4},{6,7},{7,6},{8,9},{9,8},{10,11... | collective-permute-start | bytes 3538952 | tf_op jit(solution)/shard_map/ppermute | solution.py:78
  943.2 52.9 %collective-permute-start.7 = (bf16[1,768,768]{2,1,0:T(8,128)(2,1)}, bf16[1,768,768]{2,1,0:T(8,128)(2,1)}, u32[]{:S(2)}, u32[]{:S(2)}) collective-permute-start(bf16[1,768,768]{2,1,0:T(8,128)(2,1)} %bitcast.347), channel_id=1, source_target_pairs={{0,2},{1,3},{2,0},{3,1},{4,6},{5,7},{6,4},{7,5},{8,10},{9,11},{10,... | collective-permute-start | bytes 3538952 | tf_op jit(solution)/shard_map/ppermute | solution.py:78
  944.7 51.4 %collective-permute-start.8 = (bf16[1,768,768]{2,1,0:T(8,128)(2,1)}, bf16[1,768,768]{2,1,0:T(8,128)(2,1)}, u32[]{:S(2)}, u32[]{:S(2)}) collective-permute-start(bf16[1,768,768]{2,1,0:T(8,128)(2,1)} %bitcast.342), channel_id=1, source_target_pairs={{0,3},{1,2},{2,1},{3,0},{4,7},{5,6},{6,5},{7,4},{8,11},{9,10},{10,... | collective-permute-start | bytes 3538952 | tf_op jit(solution)/shard_map/ppermute | solution.py:78
  1005.2 8.1 copy-start.5
  1222.5 7.8 copy-start.6
  1222.5 7.8 copy-start.11
  1271.2 29.1 %collective-permute-start.9 = (bf16[1,768,768]{2,1,0:T(8,128)(2,1)}, bf16[1,768,768]{2,1,0:T(8,128)(2,1)S(1)}, u32[]{:S(2)}, u32[]{:S(2)}) collective-permute-start(bf16[1,768,768]{2,1,0:T(8,128)(2,1)} %bitcast.352), channel_id=1, source_target_pairs={{0,1},{1,0},{2,3},{3,2},{4,5},{5,4},{6,7},{7,6},{8,9},{9,8},{10,11... | collective-permute-start | bytes 3538952 | tf_op jit(solution)/shard_map/ppermute | solution.py:78
  1272.1 48.9 %collective-permute-start.10 = (bf16[1,768,768]{2,1,0:T(8,128)(2,1)}, bf16[1,768,768]{2,1,0:T(8,128)(2,1)}, u32[]{:S(2)}, u32[]{:S(2)}) collective-permute-start(bf16[1,768,768]{2,1,0:T(8,128)(2,1)} %bitcast.348), channel_id=1, source_target_pairs={{0,2},{1,3},{2,0},{3,1},{4,6},{5,7},{6,4},{7,5},{8,10},{9,11},{10,... | collective-permute-start | bytes 3538952 | tf_op jit(solution)/shard_map/ppermute | solution.py:78
  1272.7 50.0 %collective-permute-start.11 = (bf16[1,768,768]{2,1,0:T(8,128)(2,1)}, bf16[1,768,768]{2,1,0:T(8,128)(2,1)}, u32[]{:S(2)}, u32[]{:S(2)}) collective-permute-start(bf16[1,768,768]{2,1,0:T(8,128)(2,1)} %bitcast.343), channel_id=1, source_target_pairs={{0,3},{1,2},{2,1},{3,0},{4,7},{5,6},{6,5},{7,4},{8,11},{9,10},{10,... | collective-permute-start | bytes 3538952 | tf_op jit(solution)/shard_map/ppermute | solution.py:78
  (6 other events, 45.8 us)
Sparse Core Ops, SparseCore 0:
  679.8 196.1 all-reduce.10
  1546.0 195.4 all-reduce.12
